TPU v7x, 128 devices: a whole 4x4x4 slice. The times are simulated.
128 devices in a mesh: ctl: 32 (over y, z_lo, x), side: 2 (over core), tp: 2 (over z_hi).
Axes of the slice: x: 4, y: 4, z: 4 (z_hi: 2, z_lo: 2; z = z_hi * 2 + z_lo), core: 2. Of those that a mesh axis runs over, the one named last changes fastest.
Arguments:
- image_latent: bfloat16 [64, 256, 3072], P('ctl'), may hold values from -6 to 6
- control_latent: bfloat16 [64, 256, 3072], P('ctl'), may hold values from -6 to 6
- control_order: int32 [64, 256], P('ctl'), may hold values from 0 to 255, each once within a row
- captions: bfloat16 [128, 128, 3072], P('ctl'), may hold values from -6 to 6
- caption_ids: int32 [64], P('ctl'), may hold values from 0 to 3
- modulation: float32 [2, 64, 3, 3072], P('side', 'ctl'), may hold values from -3 to 3
- qkv_weight: bfloat16 [2, 3072, 3, 1536], P('side', 'ctl', None, 'tp'), may hold values from -1 to 1
- qk_gain: float32 [2, 2, 128], P('side'), may hold values from 1 to 6
- out_weight: bfloat16 [2, 1536, 3072], P('side', 'tp', 'ctl'), may hold values from -0.5 to 0.5
- zero_weight: bfloat16 [3072, 3072], P('ctl', 'tp'), may hold values from -0.109375 to 0.109375
- proj_weight: bfloat16 [3072, 64], P('tp'), may hold values from -1 to 1
- final_mod: float32 [64, 2, 3072], P('ctl'), may hold values from -3 to 3
- velocity_target: float32 [64, 256, 64], P('ctl'), may hold values from -6 to 6
Outputs:
- hidden_out: bfloat16 [2, 64, 256, 3072], P('side', 'ctl', None, 'tp')
- zero_grad: float32 [3072, 3072], P(('ctl', 'side'), 'tp')
Inputs may be any that keep to these rules, and one draw needn't show every extreme that they name: caption_ids counts from the first caption held by the sample's own index of ctl. Each sample's row of control_order is a permutation.
All inputs are finite; a program needn't handle non-finite values.
Results may differ from a plain program's by a relative error of at most 0.03.
Values may be sent and summed in bfloat16 or wider, within the bound.
No kernel may reach another device: no remote copies, remote signals or barrier semaphores. Data moves between devices by JAX's collectives and lax.ppermute only.
A program may use at most 192 MiB of HBM per device.

v0:
```python
import math
import jax
import jax.numpy as jnp
from jax import lax
from jax.sharding import PartitionSpec as P

HEAD_DIM = 128
EPS = 1e-06


def passed_along(shard, axis, by):
    length = lax.axis_size(axis)
    pairs = [(i, i + by) for i in range(length) if 0 <= i + by < length]
    return lax.ppermute(shard, axis, pairs)


def partner(value, axis, bit):
    mask = 2**bit
    pairs = [(source, source ^ mask) for source in range(lax.axis_size(axis))]
    return lax.ppermute(value, axis, pairs)


def layer_norm(values):
    center = values - jnp.mean(values, axis=-1, keepdims=True)
    spread = jnp.mean(center * center, axis=-1, keepdims=True)
    return center * lax.rsqrt(spread + EPS)


def head_norm(values, gain_row):
    power_mean = jnp.mean(values * values, axis=-1, keepdims=True)
    return (values * lax.rsqrt(power_mean + EPS) * gain_row).astype(jnp.bfloat16)


def rounded(values):
    narrow = lax.optimization_barrier(values.astype(jnp.bfloat16))
    return narrow.astype(jnp.float32)


def local(
    image_latent,
    control_latent,
    control_order,
    captions,
    caption_ids,
    modulation,
    qkv_weight,
    qk_gain,
    out_weight,
    zero_weight,
    proj_weight,
    final_mod,
    velocity_target,
):
    side_index = lax.axis_index("side")
    tp_index = lax.axis_index("tp")
    ctl_count = lax.axis_size("ctl")
    tp_count = lax.axis_size("tp")
    is_control = side_index == 0
    micro_count, img_rows, width_full = image_latent.shape
    text_rows = captions.shape[1]
    seq_rows = text_rows + img_rows
    local_heads = qkv_weight.shape[3]
    head_count = local_heads // HEAD_DIM
    half_width = width_full // tp_count
    quarter_width = half_width // 2
    flat_rows = micro_count * img_rows
    block_rows = width_full // (2 * ctl_count)
    aligned = jax.vmap(lambda latent, order_row: jnp.take(latent, order_row, axis=0))(
        control_latent, control_order
    )
    plain_rows = image_latent.astype(jnp.float32)
    hidden = plain_rows + jnp.where(is_control, 1.0, 0.0) * aligned.astype(jnp.float32)
    chosen = jnp.take(captions, caption_ids, axis=0).astype(jnp.float32)
    sequence = jnp.concatenate([chosen, hidden], axis=1)
    modulate = modulation[0]
    normed = (layer_norm(sequence) * (1.0 + modulate[:, 1:2]) + modulate[:, 0:1]).astype(
        jnp.bfloat16
    )
    text_flat = normed.reshape(micro_count * seq_rows, width_full)
    image_flat = normed[:, text_rows:].reshape(flat_rows, width_full)
    shard_piece = lax.all_gather(qkv_weight, "ctl", axis=1, tiled=True)
    count_rows = shard_piece.shape[1]
    query_acc = jnp.dot(image_flat, shard_piece[0, :, 0], preferred_element_type=jnp.float32)
    pair_weight = shard_piece[0, :, 1:].reshape(count_rows, 2 * local_heads)
    pair_acc = jnp.dot(text_flat, pair_weight, preferred_element_type=jnp.float32)
    query_acc, pair_acc = (query_acc, pair_acc)
    gain_pair = qk_gain[0]
    queries = head_norm(
        query_acc.reshape(micro_count, img_rows, head_count, HEAD_DIM), gain_pair[0]
    )
    pair_acc = pair_acc.reshape(micro_count, seq_rows, 2, head_count, HEAD_DIM)
    keys_all = head_norm(pair_acc[:, :, 0], gain_pair[1])
    values_all = pair_acc[:, :, 1].astype(jnp.bfloat16)
    scores = jnp.einsum(
        "bihd,bjhd->bhij", queries, keys_all, preferred_element_type=jnp.float32
    ) / math.sqrt(HEAD_DIM)
    attend = jax.nn.softmax(scores, axis=-1).astype(jnp.bfloat16)
    mixed_heads = jnp.einsum(
        "bhij,bjhd->bihd", attend, values_all, preferred_element_type=jnp.float32
    )
    mixed_heads = mixed_heads.astype(jnp.bfloat16).reshape(flat_rows, local_heads)
    partial_value = rounded(
        jnp.dot(
            mixed_heads,
            lax.all_gather(out_weight, "ctl", axis=2, tiled=True)[0],
            preferred_element_type=jnp.float32,
        )
    )
    head_sum = lax.psum_scatter(
        partial_value.astype(jnp.bfloat16), "tp", scatter_dimension=1, tiled=True
    ).astype(jnp.float32)
    hid_half = lax.dynamic_slice_in_dim(hidden, tp_index * half_width, half_width, 2)
    gate_half = lax.dynamic_slice_in_dim(modulate[:, 2:3], tp_index * half_width, half_width, 2)
    act_half = hid_half + gate_half * head_sum.reshape(micro_count, img_rows, half_width)
    act_half = act_half.reshape(flat_rows, half_width)
    act_narrow = lax.all_gather(act_half.astype(jnp.bfloat16), "tp", axis=1, tiled=True)
    act_other = passed_along(act_narrow, "side", 1)
    control_rows = jnp.where(is_control, act_narrow, act_other)
    own_cols = lax.dynamic_slice_in_dim(zero_weight, side_index * quarter_width, quarter_width, 1)
    columns = control_rows
    own_part = jnp.dot(
        columns,
        lax.all_gather(own_cols, "ctl", axis=0, tiled=True),
        preferred_element_type=jnp.float32,
    )
    own_narrow = own_part.astype(jnp.bfloat16)
    other_narrow = partner(own_narrow, "side", 0)
    residual_narrow = jnp.where(
        is_control,
        jnp.concatenate([own_narrow, other_narrow], axis=1),
        jnp.concatenate([other_narrow, own_narrow], axis=1),
    )
    merged = act_half + residual_narrow.astype(jnp.float32)
    section_out = jnp.where(is_control, residual_narrow, merged.astype(jnp.bfloat16))
    final_half = lax.dynamic_slice_in_dim(final_mod, tp_index * half_width, half_width, 2)
    merged_rows = merged.reshape(micro_count, img_rows, half_width)
    row_total, squares = lax.psum(
        (
            jnp.sum(merged_rows, axis=-1, keepdims=True),
            jnp.sum(merged_rows * merged_rows, axis=-1, keepdims=True),
        ),
        "tp",
    )
    mean_val = row_total / width_full
    spread = squares / width_full - mean_val * mean_val
    scale_inv = lax.rsqrt(spread + EPS)
    unit_rows = (merged_rows - mean_val) * scale_inv
    final_in = (unit_rows * (1.0 + final_half[:, 1:2]) + final_half[:, 0:1]).astype(jnp.bfloat16)
    prediction = lax.psum(
        jnp.dot(
            final_in.reshape(flat_rows, half_width), proj_weight, preferred_element_type=jnp.float32
        ).astype(jnp.bfloat16),
        "tp",
    ).astype(jnp.float32)
    loss_factor = 4.0 / math.sqrt(micro_count * ctl_count * img_rows)
    grad_pred = (loss_factor * (prediction - velocity_target.reshape(flat_rows, -1))).astype(
        jnp.bfloat16
    )
    grad_unit = lax.dot_general(
        grad_pred, proj_weight, (((1,), (1,)), ((), ())), preferred_element_type=jnp.float32
    )
    grad_unit = grad_unit.reshape(micro_count, img_rows, half_width) * (1.0 + final_half[:, 1:2])
    first_sum, second_sum = lax.psum(
        (
            jnp.sum(grad_unit, axis=-1, keepdims=True),
            jnp.sum(grad_unit * unit_rows, axis=-1, keepdims=True),
        ),
        "tp",
    )
    grad_narrow = (
        (grad_unit - first_sum / width_full - unit_rows * (second_sum / width_full)) * scale_inv
    ).astype(jnp.bfloat16)
    grad_narrow = grad_narrow.reshape(flat_rows, half_width)
    returned = passed_along(grad_narrow, "side", -1)
    grad_rows_all = jnp.where(is_control, returned, grad_narrow)
    own_act = lax.dynamic_index_in_dim(
        control_rows.reshape(flat_rows, ctl_count, 2, block_rows), side_index, 2, keepdims=False
    )
    own_act = own_act.reshape(flat_rows, ctl_count * block_rows)
    columns = own_act
    product = lax.dot_general(
        columns, grad_rows_all, (((0,), (0,)), ((), ())), preferred_element_type=jnp.float32
    )
    zero_grad = lax.psum_scatter(
        rounded(product).astype(jnp.bfloat16), "ctl", scatter_dimension=0, tiled=True
    ).astype(jnp.float32)
    return (section_out.reshape(1, micro_count, img_rows, half_width), zero_grad)


def solution(mesh):
    return jax.shard_map(
        local,
        mesh=mesh,
        in_specs=(
            P("ctl", None, None),
            P("ctl", None, None),
            P("ctl", None),
            P("ctl", None, None),
            P("ctl"),
            P("side", "ctl", None, None),
            P("side", "ctl", None, "tp"),
            P("side", None, None),
            P("side", "tp", "ctl"),
            P("ctl", "tp"),
            P("tp", None),
            P("ctl", None, None),
            P("ctl", None, None),
        ),
        out_specs=(P("side", "ctl", None, "tp"), P(("ctl", "side"), "tp")),
        check_vma=False,
    )
```

profile of v0, /device:TPU:0, one launch (start us, length us, event | category | flops | bytes accessed | tf_op | source)
XLA Modules:
  0.0 868.4 jit_solution(13904714863020489514)
XLA Ops:
  11.4 0.8 slice_bitcast_fusion.6
  12.2 14.7 %gather_fusion.1 = bf16[512,3072]{1,0:T(8,128)(2,1)} fusion(bf16[2,256,3072]{2,1,0:T(8,128)(2,1)S(1)} %copy-done, s32[512]{0:T(512)S(1)} %bitcast.114), kind=kCustom, calls=%fused_computation.1 | custom fusion | bytes 6295552 | tf_op jit(solution)/shard_map/vmap(jit(_take))/gather | solution.py:68
  26.9 7.2 multiply_add_fusion
  34.1 1.8 gather_fusion
  35.9 1.9 select_convert_fusion
  37.8 3.5 fusion.1
  41.4 1.3 multiply_reduce_fusion
  42.7 3.7 add_convert_fusion
  46.4 144.6 %all-gather.5.cloned.1.call-done = bf16[1,3072,3,768]{3,1,2,0:T(8,128)(2,1)} async-done(((bf16[1,96,3,768]{3,1,2,0:T(8,128)(2,1)}), bf16[1,3072,3,768]{3,1,2,0:T(8,128)(2,1)}) %all-gather.5.cloned.1.call-update) | async-done | bytes 14155792 | tf_op jit(solution)/shard_map/all_gather | solution.py:81
  191.0 7.8 slice.59
  198.9 12.7 %copy.37 = bf16[1,3072,2,768]{1,3,2,0:T(8,128)(2,1)} copy(bf16[1,3072,2,768]{3,1,2,0:T(8,128)(2,1)} %slice.59) | data formatting | bytes 18874368
  211.5 4.8 slice_bitcast_fusion
  216.3 6.7 copy.25
  223.0 11.8 %fusion.2 = f32[2,384,2,6,128]{1,4,3,2,0:T(8,128)S(1)} fusion(bf16[2,6,128,3072,1]{3,2,1,0,4:T(8,128)(2,1)} %bitcast.117, bf16[2,384,3072]{2,1,0:T(8,128)(2,1)} %add_convert_fusion), kind=kOutput, calls=%fused_computation.10 | convolution fusion | flops 7247757312 | bytes 18874368 | tf_op jit(solution)/shard_map/dot_general | solution.py:85
  235.1 6.0 multiply_reduce_fusion.5
  241.1 0.9 fusion.22
  242.1 2.1 copy-done.3
  244.2 1.7 fusion.44
  245.9 10.0 %fusion.21 = bf16[2,256,6,128]{1,3,2,0:T(8,128)(2,1)S(1)} fusion(f32[2,6,256]{2,1,0:T(8,128)S(1)} %fusion.44, f32[2,384,2,6,128]{1,4,3,2,0:T(8,128)} %copy-done.7, f32[2,6,256,384]{3,2,1,0:T(8,128)} %copy-done.3), kind=kOutput, calls=%fused_computation.48 | convolution fusion | flops 308284800 | bytes 11415552 | tf_op jit(solution)/shard_map/bhij,bjhd->bihd/dot_general | solution.py:98
  256.0 0.8 copy.28
  257.0 91.9 %all-gather.7.cloned.1.call-done = bf16[1,768,3072]{1,2,0:T(8,128)(2,1)} async-done(((bf16[1,768,96]{1,2,0:T(8,128)(2,1)}), bf16[1,768,3072]{1,2,0:T(8,128)(2,1)}) %all-gather.7.cloned.1.call-update) | async-done | bytes 4718608 | tf_op jit(solution)/shard_map/all_gather | solution.py:105
  348.9 6.4 fusion.6
  355.4 47.4 %reduce-scatter.3.cloned.1.call-done = bf16[512,1536]{1,0:T(8,128)(2,1)} async-done(((bf16[512,3072]{1,0:T(8,128)(2,1)}), bf16[512,1536]{1,0:T(8,128)(2,1)}) %reduce-scatter.3.cloned.1.call-update) | async-done | bytes 1572880 | tf_op jit(solution)/shard_map/reduce_scatter | solution.py:109
  402.8 2.8 fusion.17
  405.6 1.8 copy.29
  408.3 47.6 %all-gather.9.cloned.1.call-done = bf16[512,3072]{0,1:T(8,128)(2,1)} async-done(((bf16[512,1536]{0,1:T(8,128)(2,1)}), bf16[512,3072]{0,1:T(8,128)(2,1)}) %all-gather.9.cloned.1.call-update) | async-done | bytes 3145744 | tf_op jit(solution)/shard_map/all_gather | solution.py:116
  455.9 1.8 collective-permute-start
  457.7 5.3 collective-permute-done
  463.0 2.3 broadcast_select_fusion
  465.3 149.6 %all-gather.11.cloned.1.call-done = bf16[3072,768]{1,0:T(8,128)(2,1)} async-done(((bf16[96,768]{1,0:T(8,128)(2,1)}), bf16[3072,768]{1,0:T(8,128)(2,1)}) %all-gather.11.cloned.1.call-update) | async-done | bytes 4718608 | tf_op jit(solution)/shard_map/all_gather | solution.py:123
  614.9 5.9 convolution_convert_fusion.1
  620.9 2.5 collective-permute-done.1
  623.4 3.9 fusion.42
  627.3 6.6 all-reduce.1
  634.6 1.2 convolution_convert_fusion.2
  635.9 0.9 copy.38
  636.8 28.0 %all-reduce.4.cloned.1.call-done = bf16[512,64]{0,1:T(8,128)(2,1)} async-done(((bf16[512,64]{0,1:T(8,128)(2,1)}), bf16[512,64]{0,1:T(8,128)(2,1)}) %all-reduce.4.cloned.1.call-update) | async-done | bytes 65552 | tf_op jit(solution)/shard_map/psum | solution.py:149
  664.8 1.5 fusion.14
  667.0 1.0 copy-done.4
  668.0 6.4 all-reduce
  674.4 4.0 multiply_convert_fusion
  678.4 1.3 collective-permute-start.2
  679.7 1.5 constant_dynamic-slice_fusion.1
  681.2 2.7 collective-permute-done.2
  683.9 4.2 convolution_convert_fusion
  688.2 4.7 select_bitcast_fusion
  692.8 167.0 %reduce-scatter.5.cloned.1.call-done = bf16[48,1536]{1,0:T(8,128)(2,1)} async-done(((bf16[1536,1536]{1,0:T(8,128)(2,1)}), bf16[48,1536]{1,0:T(8,128)(2,1)}) %reduce-scatter.5.cloned.1.call-update) | async-done | bytes 147472 | tf_op jit(solution)/shard_map/reduce_scatter | solution.py:184
  859.9 1.6 convert_element_type.110
  (67 shorter events, 7.2 us)
Async XLA Ops:
  7.2 5.0 copy-start
  7.2 183.8 %all-gather.5.cloned.1.call-start = ((), (), s32[]{:S(2)}) async-start(), calls=%async_computation.2 | async-start | bytes 14598144 | tf_op jit(solution)/shard_map/all_gather | solution.py:81
  7.9 340.9 %all-gather.7.cloned.1.call-start = ((), (), s32[]{:S(2)}) async-start(), calls=%async_computation.3 | async-start | bytes 4866048 | tf_op jit(solution)/shard_map/all_gather | solution.py:105
  8.7 394.1 %reduce-scatter.3.cloned.1.call-start = ((), (), s32[]{:S(2)}) async-start(), calls=%async_computation.4 | async-start | bytes 4718592 | tf_op jit(solution)/shard_map/reduce_scatter | solution.py:109
  26.9 7.2 copy-start.8
  35.9 5.4 slice-start
  37.8 3.7 slice-start.1
  41.4 1.3 copy-start.11
  223.0 12.1 %copy-start.6 = (bf16[768,3072]{1,0:T(8,128)(2,1)S(1)}, bf16[768,3072]{1,0:T(8,128)(2,1)}, u32[]{:S(2)}) copy-start(bf16[768,3072]{1,0:T(8,128)(2,1)} %copy.25) | copy-start | bytes 14155780
  234.9 6.3 copy-start.7
  242.1 2.1 copy-start.3
  355.3 100.6 %all-gather.9.cloned.1.call-start = ((), (), s32[]{:S(2)}) async-start(), calls=%async_computation.5 | async-start | bytes 4718592 | tf_op jit(solution)/shard_map/all_gather | solution.py:116
  405.6 1.9 copy-start.10
  407.5 207.4 %all-gather.11.cloned.1.call-start = ((), (), s32[]{:S(2)}) async-start(), calls=%async_computation.6 | async-start | bytes 4866048 | tf_op jit(solution)/shard_map/all_gather | solution.py:123
  408.2 256.6 %all-reduce.4.cloned.1.call-start = ((), (), s32[]{:S(2)}) async-start(), calls=%async_computation.7 | async-start | bytes 131072 | tf_op jit(solution)/shard_map/psum | solution.py:149
  455.9 7.0 collective-permute-start
  465.3 155.5 %copy-start.5 = (bf16[512,3072]{0,1:T(8,128)(2,1)}, bf16[512,3072]{0,1:T(8,128)(2,1)S(1)}, u32[]{:S(2)}) copy-start(bf16[512,3072]{0,1:T(8,128)(2,1)S(1)} %broadcast_select_fusion) | copy-start | bytes 9437188
  465.3 155.5 %copy-start.12 = (f32[2,2,3072]{2,1,0:T(2,128)S(1)}, f32[2,2,3072]{2,1,0:T(2,128)}, u32[]{:S(2)}) copy-start(f32[2,2,3072]{2,1,0:T(2,128)} %param.24) | copy-start | bytes 147460
  620.8 2.6 collective-permute-start.1
  627.3 47.1 %copy-start.2 = (f32[2,256,1536]{2,1,0:T(8,128)}, f32[2,256,1536]{2,1,0:T(8,128)S(1)}, u32[]{:S(2)}) copy-start(f32[2,256,1536]{2,1,0:T(8,128)S(1)} %get-tuple-element.8) | copy-start | bytes 9437188
  627.3 7.2 copy-start.9
  635.8 224.0 %reduce-scatter.5.cloned.1.call-start = ((), (), s32[]{:S(2)}) async-start(), calls=%async_computation.8 | async-start | bytes 4866048 | tf_op jit(solution)/shard_map/reduce_scatter | solution.py:184
  666.3 1.7 copy-start.4
  678.4 5.5 collective-permute-start.2
  688.1 173.4 %copy-start.1 = (bf16[2,256,3072]{2,1,0:T(8,128)(2,1)S(1)}, bf16[2,256,3072]{2,1,0:T(8,128)(2,1)}, u32[]{:S(2)}) copy-start(bf16[2,256,3072]{2,1,0:T(8,128)(2,1)} %param.14) | copy-start | bytes 9437188
Sparse Core Ops, SparseCore 0:
  9.6 181.3 all-gather.4
  192.7 156.1 all-gather.6
  355.4 47.3 reduce-scatter.2
  407.6 48.2 all-gather.8
  458.0 156.8 all-gather.10
  635.9 28.8 all-reduce.3
  688.3 171.5 reduce-scatter.4
where the time goes:
time: 869 us; the launch traced here: 868 us
  waiting for transfers between devices  688 us (79%)
  local copies, waits for them, and re-layouts  58.5 us (7%)
  matrix products  48.1 us (6%)
  other arithmetic  42.8 us (5%)
  between operations  14.5 us (2%)
  blocking collectives  13 us (1%)
    reduce_scatter x1, waiting for transfers between devices, local(): lax.psum_scatter(rounded(product).astype(jnp.bfloat16), 'ctl', scatter_di...  167 us
    all_gather x1, waiting for transfers between devices, local(): lax.all_gather(own_cols, 'ctl', axis=0, tiled=True)  150 us
    all_gather x1, waiting for transfers between devices, local(): shard_piece = lax.all_gather(qkv_weight, 'ctl', axis=1, tiled=True)  145 us
    all_gather x1, waiting for transfers between devices, local(): lax.all_gather(out_weight, 'ctl', axis=2, tiled=True)[0]  91.9 us
    all_gather x1, waiting for transfers between devices, local(): lax.all_gather(act_half.astype(jnp.bfloat16), 'tp', axis=1, tiled=True)  47.6 us
    reduce_scatter x1, waiting for transfers between devices, local(): lax.psum_scatter(partial_value.astype(jnp.bfloat16), 'tp', scatter_dimens...  47.4 us
    psum x1, waiting for transfers between devices, local(): lax.psum(jnp.dot(final_in.reshape(flat_rows, half_width), proj_weight, pr...  28 us
  transfers between devices with their start and end apart: 10, of which 10 were waited for; matrix products, arithmetic and copies ran while one was open for 13% of the time, Pallas kernels for 0%

commit v1 on v0

--- a/solution.py
+++ b/solution.py
@@ -118,10 +118,11 @@
     control_rows = jnp.where(is_control, act_narrow, act_other)
     own_cols = lax.dynamic_slice_in_dim(zero_weight, side_index * quarter_width, quarter_width, 1)
     columns = control_rows
+    scan_stops_all_over_axis = lambda obj: jnp.concatenate(
+        lax.all_to_all(jnp.stack(lax.axis_size("ctl") * [obj]), "ctl", 0, 0), axis=0
+    )
     own_part = jnp.dot(
-        columns,
-        lax.all_gather(own_cols, "ctl", axis=0, tiled=True),
-        preferred_element_type=jnp.float32,
+        columns, scan_stops_all_over_axis(own_cols), preferred_element_type=jnp.float32
     )
     own_narrow = own_part.astype(jnp.bfloat16)
     other_narrow = partner(own_narrow, "side", 0)

time: 869 us -> 771 us (0.89)
  waiting for transfers between devices: 688 us -> 579 us
    all_gather x1 -> x0, waiting for transfers between devices: 150 us -> none  [local(): lax.all_gather(own_cols, 'ctl', axis=0, tiled=True)]
    all_gather x1, waiting for transfers between devices: 47.6 us -> 86.6 us  [local(): lax.all_gather(act_half.astype(jnp.bfloat16), 'tp', axis=1, tiled=True)]
  transfers between devices with their start and end apart: 10 -> 10, of which waited for: 10 -> 9; matrix products, arithmetic and copies ran while one was open for 13% -> 15% of each run, Pallas kernels for 0% -> 0%
where the time goes in v1:
time: 771 us; the launch traced here: 770 us
  waiting for transfers between devices  579 us (75%)
  local copies, waits for them, and re-layouts  60.6 us (8%)
  matrix products  49.3 us (6%)
  other arithmetic  42.9 us (6%)
  between operations  14.5 us (2%)
  blocking collectives  13 us (2%)
  starting transfers between devices  10.9 us (1%)
    reduce_scatter x1, waiting for transfers between devices, local(): lax.psum_scatter(rounded(product).astype(jnp.bfloat16), 'ctl', scatter_di...  167 us
    all_gather x1, waiting for transfers between devices, local(): shard_piece = lax.all_gather(qkv_weight, 'ctl', axis=1, tiled=True)  145 us
    all_gather x1, waiting for transfers between devices, local(): lax.all_gather(out_weight, 'ctl', axis=2, tiled=True)[0]  91.6 us
    all_gather x1, waiting for transfers between devices, local(): lax.all_gather(act_half.astype(jnp.bfloat16), 'tp', axis=1, tiled=True)  86.6 us
    reduce_scatter x1, waiting for transfers between devices, local(): lax.psum_scatter(partial_value.astype(jnp.bfloat16), 'tp', scatter_dimens...  47.8 us
    psum x1, waiting for transfers between devices, local(): lax.psum(jnp.dot(final_in.reshape(flat_rows, half_width), proj_weight, pr...  28.6 us
    unnamed x34, local copies, waits for them, and re-layouts  16.2 us
  transfers between devices with their start and end apart: 10, of which 9 were waited for; matrix products, arithmetic and copies ran while one was open for 15% of the time, Pallas kernels for 0%

profile of v1, /device:TPU:0, one launch (start us, length us, event | category | flops | bytes accessed | tf_op | source)
XLA Modules:
  0.0 769.7 jit_solution(9345542139527392135)
XLA Ops:
  12.2 14.8 %gather_fusion.1 = bf16[512,3072]{1,0:T(8,128)(2,1)} fusion(bf16[2,256,3072]{2,1,0:T(8,128)(2,1)S(1)} %copy-done, s32[512]{0:T(512)S(1)} %bitcast.115), kind=kCustom, calls=%fused_computation.1 | custom fusion | bytes 6295552 | tf_op jit(solution)/shard_map/vmap(jit(_take))/gather | solution.py:68
  26.9 7.2 multiply_add_fusion
  34.1 1.8 gather_fusion
  35.9 1.9 select_convert_fusion
  37.8 3.5 fusion.1
  41.4 1.3 multiply_reduce_fusion
  42.7 3.7 add_convert_fusion
  46.4 145.0 %all-gather.4.cloned.1.call-done = bf16[1,3072,3,768]{3,1,2,0:T(8,128)(2,1)} async-done(((bf16[1,96,3,768]{3,1,2,0:T(8,128)(2,1)}), bf16[1,3072,3,768]{3,1,2,0:T(8,128)(2,1)}) %all-gather.4.cloned.1.call-update) | async-done | bytes 14155792 | tf_op jit(solution)/shard_map/all_gather | solution.py:81
  191.5 7.9 %slice.59 = bf16[1,3072,2,768]{3,1,2,0:T(8,128)(2,1)} slice(bf16[1,3072,3,768]{3,1,2,0:T(8,128)(2,1)} %all-gather.4.cloned.1.call-done), slice={[0:1], [0:3072], [1:3], [0:768]} | slice | bytes 18874368 | tf_op jit(solution)/shard_map/slice | solution.py:84
  199.3 12.7 %copy.37 = bf16[1,3072,2,768]{1,3,2,0:T(8,128)(2,1)} copy(bf16[1,3072,2,768]{3,1,2,0:T(8,128)(2,1)} %slice.59) | data formatting | bytes 18874368
  212.0 4.8 slice_bitcast_fusion
  216.8 6.7 copy.25
  223.5 11.8 %fusion.2 = f32[2,384,2,6,128]{1,4,3,2,0:T(8,128)S(1)} fusion(bf16[2,6,128,3072,1]{3,2,1,0,4:T(8,128)(2,1)} %bitcast.118, bf16[2,384,3072]{2,1,0:T(8,128)(2,1)} %add_convert_fusion), kind=kOutput, calls=%fused_computation.10 | convolution fusion | flops 7247757312 | bytes 18874368 | tf_op jit(solution)/shard_map/dot_general | solution.py:85
  235.5 6.0 multiply_reduce_fusion.5
  241.6 0.9 fusion.22
  242.5 2.1 copy-done.3
  244.7 1.7 fusion.44
  246.4 10.0 %fusion.21 = bf16[2,256,6,128]{1,3,2,0:T(8,128)(2,1)S(1)} fusion(f32[2,6,256]{2,1,0:T(8,128)S(1)} %fusion.44, f32[2,384,2,6,128]{1,4,3,2,0:T(8,128)} %copy-done.7, f32[2,6,256,384]{3,2,1,0:T(8,128)} %copy-done.3), kind=kOutput, calls=%fused_computation.48 | convolution fusion | flops 308284800 | bytes 11415552 | tf_op jit(solution)/shard_map/bhij,bjhd->bihd/dot_general | solution.py:98
  256.4 0.8 copy.28
  257.4 91.6 %all-gather.6.cloned.1.call-done = bf16[1,768,3072]{1,2,0:T(8,128)(2,1)} async-done(((bf16[1,768,96]{1,2,0:T(8,128)(2,1)}), bf16[1,768,3072]{1,2,0:T(8,128)(2,1)}) %all-gather.6.cloned.1.call-update) | async-done | bytes 4718608 | tf_op jit(solution)/shard_map/all_gather | solution.py:105
  349.0 6.4 fusion.6
  355.5 47.8 %reduce-scatter.3.cloned.1.call-done = bf16[512,1536]{1,0:T(8,128)(2,1)} async-done(((bf16[512,3072]{1,0:T(8,128)(2,1)}), bf16[512,1536]{1,0:T(8,128)(2,1)}) %reduce-scatter.3.cloned.1.call-update) | async-done | bytes 1572880 | tf_op jit(solution)/shard_map/reduce_scatter | solution.py:109
  403.3 2.8 fusion.17
  406.1 1.8 copy.29
  408.0 2.7 stack.2
  410.7 7.3 all-to-all-start
  418.0 86.6 %all-gather.8.cloned.1.call-done = bf16[512,3072]{0,1:T(8,128)(2,1)} async-done(((bf16[512,1536]{0,1:T(8,128)(2,1)}), bf16[512,3072]{0,1:T(8,128)(2,1)}) %all-gather.8.cloned.1.call-update) | async-done | bytes 3145744 | tf_op jit(solution)/shard_map/all_gather | solution.py:116
  504.6 2.1 collective-permute-start
  506.7 5.3 collective-permute-done
  512.0 2.3 broadcast_select_fusion
  514.3 7.1 convolution_convert_fusion.1
  521.5 2.5 collective-permute-done.1
  524.0 4.0 fusion.42
  528.0 6.6 all-reduce.1
  535.3 1.2 convolution_convert_fusion.2
  536.6 0.9 copy.38
  537.5 28.6 %all-reduce.4.cloned.1.call-done = bf16[512,64]{0,1:T(8,128)(2,1)} async-done(((bf16[512,64]{0,1:T(8,128)(2,1)}), bf16[512,64]{0,1:T(8,128)(2,1)}) %all-reduce.4.cloned.1.call-update) | async-done | bytes 65552 | tf_op jit(solution)/shard_map/psum | solution.py:150
  566.1 1.5 fusion.14
  568.3 1.0 copy-done.4
  569.3 6.4 all-reduce
  575.7 4.0 multiply_convert_fusion
  579.7 1.3 collective-permute-start.2
  581.0 1.5 constant_dynamic-slice_fusion.1
  582.5 2.7 collective-permute-done.2
  585.2 4.2 convolution_convert_fusion
  589.4 4.7 select_bitcast_fusion
  594.1 167.1 %reduce-scatter.5.cloned.1.call-done = bf16[48,1536]{1,0:T(8,128)(2,1)} async-done(((bf16[1536,1536]{1,0:T(8,128)(2,1)}), bf16[48,1536]{1,0:T(8,128)(2,1)}) %reduce-scatter.5.cloned.1.call-update) | async-done | bytes 147472 | tf_op jit(solution)/shard_map/reduce_scatter | solution.py:185
  761.2 1.6 convert_element_type.110
  (67 shorter events, 7.2 us)
Async XLA Ops:
  7.2 5.0 copy-start
  7.2 184.3 %all-gather.4.cloned.1.call-start = ((), (), s32[]{:S(2)}) async-start(), calls=%async_computation.3 | async-start | bytes 14598144 | tf_op jit(solution)/shard_map/all_gather | solution.py:81
  7.9 341.0 %all-gather.6.cloned.1.call-start = ((), (), s32[]{:S(2)}) async-start(), calls=%async_computation.4 | async-start | bytes 4866048 | tf_op jit(solution)/shard_map/all_gather | solution.py:105
  8.7 394.6 %reduce-scatter.3.cloned.1.call-start = ((), (), s32[]{:S(2)}) async-start(), calls=%async_computation.5 | async-start | bytes 4718592 | tf_op jit(solution)/shard_map/reduce_scatter | solution.py:109
  26.9 7.2 copy-start.8
  35.9 5.4 slice-start
  37.8 3.7 slice-start.1
  41.4 1.3 copy-start.11
  223.5 12.1 %copy-start.6 = (bf16[768,3072]{1,0:T(8,128)(2,1)S(1)}, bf16[768,3072]{1,0:T(8,128)(2,1)}, u32[]{:S(2)}) copy-start(bf16[768,3072]{1,0:T(8,128)(2,1)} %copy.25) | copy-start | bytes 14155780
  235.3 6.3 copy-start.7
  242.5 2.1 copy-start.3
  355.4 149.2 %all-gather.8.cloned.1.call-start = ((), (), s32[]{:S(2)}) async-start(), calls=%async_computation.6 | async-start | bytes 4718592 | tf_op jit(solution)/shard_map/all_gather | solution.py:116
  406.1 1.8 copy-start.10
  410.7 103.6 %all-to-all-start = ((bf16[32,96,768]{2,1,0:T(8,128)(2,1)}), bf16[32,96,768]{2,1,0:T(8,128)(2,1)}, u32[]{:S(2)}, u32[]{:S(2)}) async-start(bf16[32,96,768]{2,1,0:T(8,128)(2,1)} %stack.2), calls=%async_computation.1 | async-start | bytes 9437184 | tf_op jit(solution)/shard_map/all_to_all | solution.py:122
  418.0 148.1 %all-reduce.4.cloned.1.call-start = ((), (), s32[]{:S(2)}) async-start(), calls=%async_computation.7 | async-start | bytes 131072 | tf_op jit(solution)/shard_map/psum | solution.py:150
  504.6 7.4 collective-permute-start
  514.3 7.1 copy-start.5
  514.3 7.1 copy-start.12
  521.4 2.6 collective-permute-start.1
  528.0 47.7 %copy-start.2 = (f32[2,256,1536]{2,1,0:T(8,128)}, f32[2,256,1536]{2,1,0:T(8,128)S(1)}, u32[]{:S(2)}) copy-start(f32[2,256,1536]{2,1,0:T(8,128)S(1)} %get-tuple-element.8) | copy-start | bytes 9437188
  528.0 7.2 copy-start.9
  536.5 224.7 %reduce-scatter.5.cloned.1.call-start = ((), (), s32[]{:S(2)}) async-start(), calls=%async_computation.8 | async-start | bytes 4866048 | tf_op jit(solution)/shard_map/reduce_scatter | solution.py:185
  567.6 1.7 copy-start.4
  579.7 5.5 collective-permute-start.2
  589.4 173.4 %copy-start.1 = (bf16[2,256,3072]{2,1,0:T(8,128)(2,1)S(1)}, bf16[2,256,3072]{2,1,0:T(8,128)(2,1)}, u32[]{:S(2)}) copy-start(bf16[2,256,3072]{2,1,0:T(8,128)(2,1)} %param.14) | copy-start | bytes 9437188
Sparse Core Ops, SparseCore 0:
  9.6 181.7 all-gather.3
  193.1 155.8 all-gather.5
  355.5 47.7 reduce-scatter.2
  408.1 96.4 all-gather.7
  536.6 29.4 all-reduce.3
  589.5 171.6 reduce-scatter.4
